TPU v7x, 512 devices: a whole 4x8x8 slice. The times are simulated.
512 devices in a mesh: ctx: 64 (over z_hi, y, core), head: 8 (over x, z_lo).
Axes of the slice: x: 4, y: 8, z: 8 (z_hi: 4, z_lo: 2; z = z_hi * 2 + z_lo), core: 2. Of those that a mesh axis runs over, the one named last changes fastest.
Arguments:
- queries: bfloat16 [65536, 8192], P(('ctx', 'head')), may hold values from -13 to 13
- keys: bfloat16 [65536, 1024], P(('ctx', 'head')), may hold values from -13 to 13
- values: bfloat16 [65536, 1024], P(('ctx', 'head')), may hold values from -6 to 6
- doc_ids: int32 [65536], replicated, may hold values from 0 to 63, never falling along the last dimension, each value on 1 to 1280 neighbouring positions
Outputs:
- attended: bfloat16 [65536, 8192], P(('ctx', 'head'))
Inputs may be any that keep to these rules, and one draw needn't show every extreme that they name: `doc_ids`: document numbers never fall along the sequence; every document has 1 to 1280 tokens and one has exactly 1280; every number of 0 to 63 occurs.
All inputs are finite; a program needn't handle non-finite values.
Results may differ from a plain program's by a relative error of at most 0.0025.
Values may be sent and summed in bfloat16 or wider, within the bound.
No kernel may reach another device: no remote copies, remote signals or barrier semaphores. Data moves between devices by JAX's collectives and lax.ppermute only.
A program may use at most 64 MiB of HBM per device.

v0:
```python
import jax
import jax.numpy as jnp
from jax import lax
from jax.sharding import PartitionSpec as P

HD = 128
QH = 64
KVH = 8
BLOCK = 256
DOC_BLOCKS = 5
QBLK_DEV = 4
PREV = 2
floor_score = -1e30


def from_behind(value, axis, steps):
    count = lax.axis_size(axis)
    leading, last = (max(0, -steps), min(count, count - steps))
    return lax.ppermute(value, axis, [(source, source + steps) for source in range(leading, last)])


def attend_tile(running, query_block, key_tile, value_tile, allowed):
    maxima, totals, accum = running
    scores = jnp.einsum(
        "qgjd,kgd->qgjk", query_block, key_tile, preferred_element_type=jnp.float32
    ) * HD ** (-0.5)
    scores = jnp.where(allowed[:, None, None, :], scores, floor_score)
    fresh = jnp.maximum(maxima, jnp.max(scores, axis=-1))
    factor = jnp.exp(maxima - fresh)
    weights = jnp.exp(scores - fresh[..., None])
    totals = totals * factor + jnp.sum(weights, axis=-1)
    accum = accum * factor[..., None] + jnp.einsum(
        "qgjk,kgd->qgjd",
        weights.astype(jnp.bfloat16),
        value_tile,
        preferred_element_type=jnp.float32,
    )
    return (fresh, totals, accum)


def key_window(paired):
    pieces = []
    for offset in range(1, PREV + 1):
        pieces.append(from_behind(paired, "ctx", offset))
    return jnp.concatenate(pieces[::-1] + [paired], axis=1)


def shards(queries, keys, values, doc_ids):
    per_group = QH // KVH
    range_rows = QBLK_DEV * BLOCK
    ctx_pos = lax.axis_index("ctx")
    local_queries, local_keys, local_values = (
        lax.all_to_all(queries, "head", split_axis=1, concat_axis=0, tiled=True),
        lax.all_to_all(keys, "head", split_axis=1, concat_axis=0, tiled=True),
        lax.all_to_all(values, "head", split_axis=1, concat_axis=0, tiled=True),
    )
    window = key_window(jnp.stack([local_keys, local_values]))
    groups = local_keys.shape[1] // HD
    window_keys = window[0].reshape(-1, groups, HD)
    window_values = window[1].reshape(-1, groups, HD)
    padded_ids = jnp.concatenate([jnp.full((PREV * range_rows,), -1, jnp.int32), doc_ids])
    window_ids = lax.dynamic_slice_in_dim(padded_ids, ctx_pos * range_rows, (PREV + 1) * range_rows)
    range_ids = lax.dynamic_slice_in_dim(doc_ids, ctx_pos * range_rows, range_rows)
    window_base = (ctx_pos - PREV) * range_rows
    offsets = jnp.arange(BLOCK, dtype=jnp.int32)
    shaped_queries = local_queries.reshape(range_rows, groups, per_group, HD)
    outputs = []
    for block_index in range(QBLK_DEV):
        query_block = shaped_queries[block_index * BLOCK : (block_index + 1) * BLOCK]
        block_ids = range_ids[block_index * BLOCK : (block_index + 1) * BLOCK]
        query_pos = ctx_pos * range_rows + block_index * BLOCK + offsets

        def visit(running, tile, query_block=query_block, block_ids=block_ids, query_pos=query_pos):
            start = tile * BLOCK
            key_tile = lax.dynamic_slice_in_dim(window_keys, start, BLOCK, 0)
            value_tile = lax.dynamic_slice_in_dim(window_values, start, BLOCK, 0)
            tile_ids = lax.dynamic_slice_in_dim(window_ids, start, BLOCK)
            key_pos = window_base + start + offsets
            allowed = (block_ids[:, None] == tile_ids[None, :]) & (
                key_pos[None, :] <= query_pos[:, None]
            )
            return attend_tile(running, query_block, key_tile, value_tile, allowed)

        initial = (
            jnp.full((BLOCK, groups, per_group), floor_score, jnp.float32),
            jnp.zeros((BLOCK, groups, per_group), jnp.float32),
            jnp.zeros((BLOCK, groups, per_group, HD), jnp.float32),
        )
        diagonal = PREV * QBLK_DEV + block_index
        running = visit(initial, diagonal)

        def backward(offset, running, visit=visit, block_ids=block_ids, diagonal=diagonal):
            tile = diagonal - offset
            return visit(running, tile)

        running = lax.fori_loop(1, DOC_BLOCKS + 1, backward, running)
        maxima, totals, accum = running
        outputs.append(
            (accum / totals[..., None]).astype(jnp.bfloat16).reshape(BLOCK, groups * per_group * HD)
        )
    local_out = jnp.concatenate(outputs, axis=0)
    return lax.all_to_all(local_out, "head", split_axis=0, concat_axis=1, tiled=True)


def solution(mesh):
    in_specs = (P(("ctx", "head"), None), P(("ctx", "head"), None), P(("ctx", "head"), None), P())
    out_specs = P(("ctx", "head"), None)
    return jax.shard_map(shards, mesh=mesh, in_specs=in_specs, out_specs=out_specs, check_vma=False)
```

profile of v0, /device:TPU:128, one launch (start us, length us, event | category | flops | bytes accessed | tf_op | source)
XLA Modules:
  0.0 223.2 jit_solution(8170471879626285882)
XLA Ops:
  1.7 6.1 %all-to-all-start = ((bf16[128,8,128]{2,0,1:T(8,128)(2,1)}), bf16[128,8,128]{2,0,1:T(8,128)(2,1)S(1)}, u32[]{:S(2)}, u32[]{:S(2)}) async-start(bf16[128,8,128]{2,0,1:T(8,128)(2,1)} %copy_bitcast_fusion.2), calls=%async_computation | async-start | bytes 524288 | tf_op jit(solution)/shard_map/all_to_all | solution.py:54
  7.8 1.7 copy_bitcast_fusion.1
  9.5 5.6 %all-to-all-done = bf16[128,8,128]{2,0,1:T(8,128)(2,1)S(1)} async-done(((bf16[128,8,128]{2,0,1:T(8,128)(2,1)}), bf16[128,8,128]{2,0,1:T(8,128)(2,1)S(1)}, u32[]{:S(2)}, u32[]{:S(2)}) %all-to-all-start) | async-done | bytes 262176 | tf_op jit(solution)/shard_map/all_to_all | solution.py:54
  15.1 3.4 %all-to-all-start.2 = ((bf16[128,8,128]{2,0,1:T(8,128)(2,1)}), bf16[128,8,128]{2,0,1:T(8,128)(2,1)S(1)}, u32[]{:S(2)}, u32[]{:S(2)}) async-start(bf16[128,8,128]{2,0,1:T(8,128)(2,1)} %copy_bitcast_fusion.1), calls=%async_computation.2 | async-start | bytes 524288 | tf_op jit(solution)/shard_map/all_to_all | solution.py:55
  18.5 1.6 copy.129
  20.1 5.7 %all-to-all-done.2 = bf16[128,8,128]{2,0,1:T(8,128)(2,1)S(1)} async-done(((bf16[128,8,128]{2,0,1:T(8,128)(2,1)}), bf16[128,8,128]{2,0,1:T(8,128)(2,1)S(1)}, u32[]{:S(2)}, u32[]{:S(2)}) %all-to-all-start.2) | async-done | bytes 262176 | tf_op jit(solution)/shard_map/all_to_all | solution.py:55
  25.7 3.7 %all-to-all-start.1 = ((bf16[128,8,1024]{2,0,1:T(8,128)(2,1)}), bf16[128,8,1024]{2,0,1:T(8,128)(2,1)S(1)}, u32[]{:S(2)}, u32[]{:S(2)}) async-start(bf16[128,8,1024]{2,0,1:T(8,128)(2,1)} %bitcast.405), calls=%async_computation.1 | async-start | bytes 4194304 | tf_op jit(solution)/shard_map/all_to_all | solution.py:53
  30.4 3.5 %collective-permute-start = (bf16[2,1024,128]{2,1,0:T(8,128)(2,1)S(1)}, bf16[2,1024,128]{2,1,0:T(8,128)(2,1)S(1)}, u32[]{:S(2)}, u32[]{:S(2)}) collective-permute-start(bf16[2,1024,128]{2,1,0:T(8,128)(2,1)S(1)} %pad_maximum_fusion.1), channel_id=1, source_target_pairs={{0,16},{8,24},{16,32},{24,40},{32,48},{40,56},{48,64},{56,72},{64,... | collective-permute-start | bytes 1572872 | tf_op jit(solution)/shard_map/ppermute | solution.py:19
  33.9 1.9 collective-permute-start.1
  36.9 28.3 %collective-permute-done = bf16[2,1024,128]{2,1,0:T(8,128)(2,1)S(1)} collective-permute-done((bf16[2,1024,128]{2,1,0:T(8,128)(2,1)S(1)}, bf16[2,1024,128]{2,1,0:T(8,128)(2,1)S(1)}, u32[]{:S(2)}, u32[]{:S(2)}) %collective-permute-start) | collective-permute-done | bytes 524320 | tf_op jit(solution)/shard_map/ppermute | solution.py:19
  65.2 3.8 %collective-permute-done.1 = bf16[2,1024,128]{2,1,0:T(8,128)(2,1)S(1)} collective-permute-done((bf16[2,1024,128]{2,1,0:T(8,128)(2,1)S(1)}, bf16[2,1024,128]{2,1,0:T(8,128)(2,1)S(1)}, u32[]{:S(2)}, u32[]{:S(2)}) %collective-permute-start.1) | collective-permute-done | bytes 524320 | tf_op jit(solution)/shard_map/ppermute | solution.py:19
  70.4 1.4 copy.65
  71.8 11.9 %all-to-all-done.1 = bf16[128,8,1024]{2,0,1:T(8,128)(2,1)S(1)} async-done(((bf16[128,8,1024]{2,0,1:T(8,128)(2,1)}), bf16[128,8,1024]{2,0,1:T(8,128)(2,1)S(1)}, u32[]{:S(2)}, u32[]{:S(2)}) %all-to-all-start.1) | async-done | bytes 2097184 | tf_op jit(solution)/shard_map/all_to_all | solution.py:53
  85.8 2.5 %fusion.81 = f32[256,1,8,128]{3,0,2,1:T(8,128)} fusion(f32[256,1,8,256]{0,3,2,1:T(8,128)S(1)} %get-tuple-element.1194, f32[256,8]{0,1:T(8,128)S(1)} %get-tuple-element.1173, f32[256,8]{0,1:T(8,128)S(1)} %get-tuple-element.1171, bf16[1,1024,128]{2,1,0:T(8,128)(2,1)} %bitcast.433), kind=kOutput, calls=%fused_computation.120 | convolution fusion | flops 135528448 | bytes 3227648 | tf_op jit(solution)/shard_map/qgjk,kgd->qgjd/dot_general | solution.py:32
  88.3 1.6 copy.63
  89.9 19.6 %while.72 = (s32[]{:T(128)}, f32[256,1,8]{0,2,1:T(8,128)S(1)}, f32[256,1,8]{0,2,1:T(8,128)S(1)}, f32[256,1,8,128]{0,3,2,1:T(8,128)S(1)}, s32[256]{0:T(256)}, /*i...) while((s32[]{:T(128)}, f32[256,1,8]{0,2,1:T(8,128)S(1)}, ...), condition=%wide.region_5.6_spmd.clone, body=%wide.region_2.5_spmd.clone.sunk | while | flops 272833024 | bytes 9314543 | solution.py:96
  91.6 1.3 fusion.146
  95.5 1.3 fusion.146
  99.4 1.3 fusion.146
  103.3 1.3 fusion.146
  107.2 1.3 fusion.146
  111.8 1.3 fusion.116
  113.4 2.5 %fusion.83 = f32[256,1,8,128]{3,0,2,1:T(8,128)} fusion(f32[256,1,8,256]{0,3,2,1:T(8,128)S(1)} %get-tuple-element.1192, f32[256,8]{0,1:T(8,128)S(1)} %get-tuple-element.1176, f32[256,8]{0,1:T(8,128)S(1)} %get-tuple-element.1174, bf16[1,1024,128]{2,1,0:T(8,128)(2,1)} %bitcast.434), kind=kOutput, calls=%fused_computation.122 | convolution fusion | flops 135528448 | bytes 3227648 | tf_op jit(solution)/shard_map/qgjk,kgd->qgjd/dot_general | solution.py:32
  115.9 1.6 copy.69
  117.5 19.7 %while.73 = (s32[]{:T(128)}, f32[256,1,8]{0,2,1:T(8,128)S(1)}, f32[256,1,8]{0,2,1:T(8,128)S(1)}, f32[256,1,8,128]{0,3,2,1:T(8,128)S(1)}, s32[256]{0:T(256)}, /*i...) while((s32[]{:T(128)}, f32[256,1,8]{0,2,1:T(8,128)S(1)}, ...), condition=%wide.region_11.12_spmd.clone, body=%wide.region_8.11_spmd.clone.sunk | while | flops 272833024 | bytes 9314543 | solution.py:96
  119.1 1.3 fusion.152
  123.1 1.3 fusion.152
  127.0 1.3 fusion.152
  130.9 1.3 fusion.152
  134.9 1.3 fusion.152
  140.3 2.5 %fusion.85 = f32[256,1,8,128]{3,0,2,1:T(8,128)} fusion(f32[256,1,8,256]{0,3,2,1:T(8,128)S(1)} %get-tuple-element.1190, f32[256,8]{0,1:T(8,128)S(1)} %get-tuple-element.1179, f32[256,8]{0,1:T(8,128)S(1)} %get-tuple-element.1177, bf16[1,1024,128]{2,1,0:T(8,128)(2,1)} %bitcast.435), kind=kOutput, calls=%fused_computation.124 | convolution fusion | flops 135528448 | bytes 3227648 | tf_op jit(solution)/shard_map/qgjk,kgd->qgjd/dot_general | solution.py:32
  142.8 1.6 copy.75
  144.5 16.4 %while.74 = (s32[]{:T(128)}, f32[256,1,8]{0,2,1:T(8,128)S(1)}, f32[256,1,8]{0,2,1:T(8,128)S(1)}, f32[256,1,8,128]{0,3,2,1:T(8,128)S(1)}, s32[256]{0:T(256)S(1)},...) while((s32[]{:T(128)}, f32[256,1,8]{0,2,1:T(8,128)S(1)}, ...), condition=%wide.region_17.18_spmd.clone, body=%wide.region_14.17_spmd.clone.sunk | while | flops 272833024 | bytes 9314543 | solution.py:96
  145.4 1.3 fusion.158
  148.7 1.3 fusion.158
  152.0 1.3 fusion.158
  155.2 1.3 fusion.158
  158.5 1.3 fusion.158
  163.9 2.5 %fusion.87 = f32[256,1,8,128]{3,0,2,1:T(8,128)} fusion(f32[256,1,8,256]{0,3,2,1:T(8,128)S(1)} %get-tuple-element.1188, f32[256,8]{0,1:T(8,128)S(1)} %get-tuple-element.1182, f32[256,8]{0,1:T(8,128)S(1)} %get-tuple-element.1180, bf16[1,1024,128]{2,1,0:T(8,128)(2,1)} %bitcast.436), kind=kOutput, calls=%fused_computation.126 | convolution fusion | flops 135528448 | bytes 3227648 | tf_op jit(solution)/shard_map/qgjk,kgd->qgjd/dot_general | solution.py:32
  166.4 1.6 copy.81
  168.1 16.6 %while.75 = (s32[]{:T(128)}, f32[256,1,8]{0,2,1:T(8,128)S(1)}, f32[256,1,8]{0,2,1:T(8,128)S(1)}, f32[256,1,8,128]{0,3,2,1:T(8,128)S(1)}, s32[256]{0:T(256)S(1)},...) while((s32[]{:T(128)}, f32[256,1,8]{0,2,1:T(8,128)S(1)}, ...), condition=%wide.region_23.24_spmd.clone, body=%wide.region_20.23_spmd.clone.sunk | while | flops 272833024 | bytes 9314543 | solution.py:96
  169.2 1.3 fusion.164
  175.8 1.3 fusion.164
  179.1 1.3 fusion.164
  182.3 1.3 fusion.164
  187.1 29.6 %all_to_all.67 = bf16[8,128,1024]{2,1,0:T(8,128)(2,1)S(1)} all-to-all(bf16[8,128,1024]{2,1,0:T(8,128)(2,1)S(1)} %bitcast.406), channel_id=1, replica_groups=mesh['ctx'=64,'head'=8] {'head'}, dimensions={0} | all-to-all | bytes 4194304 | tf_op jit(solution)/shard_map/all_to_all | solution.py:102
  216.8 2.4 %copy.85 = bf16[128,8,1024]{0,2,1:T(8,128)(2,1)} copy(bf16[128,8,1024]{2,0,1:T(8,128)(2,1)S(1)} %bitcast.407) | data formatting | bytes 4194304 | tf_op jit(solution)/shard_map/all_to_all | solution.py:102
  219.1 4.1 %copy.86 = bf16[128,8192]{1,0:T(8,128)(2,1)} copy(bf16[128,8192]{0,1:T(8,128)(2,1)} %bitcast.408) | data formatting | bytes 4194304 | tf_op jit(solution)/shard_map/all_to_all | solution.py:102
  (238 shorter events, 64.0 us)
Async XLA Ops:
  0.0 1.0 copy-start
  0.0 18.5 %copy-start.2 = (bf16[128,8192]{1,0:T(8,128)(2,1)S(1)}, bf16[128,8192]{1,0:T(8,128)(2,1)}, u32[]{:S(2)}) copy-start(bf16[128,8192]{1,0:T(8,128)(2,1)} %param.12) | copy-start | bytes 6291460
  1.7 13.4 %all-to-all-start = ((bf16[128,8,128]{2,0,1:T(8,128)(2,1)}), bf16[128,8,128]{2,0,1:T(8,128)(2,1)S(1)}, u32[]{:S(2)}, u32[]{:S(2)}) async-start(bf16[128,8,128]{2,0,1:T(8,128)(2,1)} %copy_bitcast_fusion.2), calls=%async_computation | async-start | bytes 524288 | tf_op jit(solution)/shard_map/all_to_all | solution.py:54
  15.1 10.6 %all-to-all-start.2 = ((bf16[128,8,128]{2,0,1:T(8,128)(2,1)}), bf16[128,8,128]{2,0,1:T(8,128)(2,1)S(1)}, u32[]{:S(2)}, u32[]{:S(2)}) async-start(bf16[128,8,128]{2,0,1:T(8,128)(2,1)} %copy_bitcast_fusion.1), calls=%async_computation.2 | async-start | bytes 524288 | tf_op jit(solution)/shard_map/all_to_all | solution.py:55
  25.7 43.3 %copy-start.1 = (bf16[128,8,128]{2,0,1:T(8,128)(2,1)}, bf16[128,8,128]{2,0,1:T(8,128)(2,1)S(1)}, u32[]{:S(2)}) copy-start(bf16[128,8,128]{2,0,1:T(8,128)(2,1)S(1)} %all-to-all-done.2) | copy-start | bytes 786436
  25.7 3.8 %copy-start.5 = (s32[65536]{0:T(1024)S(1)}, s32[65536]{0:T(1024)}, u32[]{:S(2)}) copy-start(s32[65536]{0:T(1024)} %param.15) | copy-start | bytes 786436
  25.7 57.9 %all-to-all-start.1 = ((bf16[128,8,1024]{2,0,1:T(8,128)(2,1)}), bf16[128,8,1024]{2,0,1:T(8,128)(2,1)S(1)}, u32[]{:S(2)}, u32[]{:S(2)}) async-start(bf16[128,8,1024]{2,0,1:T(8,128)(2,1)} %bitcast.405), calls=%async_computation.1 | async-start | bytes 4194304 | tf_op jit(solution)/shard_map/all_to_all | solution.py:53
  30.3 34.9 %copy-start.11 = (s32[256]{0:T(256)}, s32[256]{0:T(256)S(1)}, u32[]{:S(2)}) copy-start(s32[256]{0:T(256)S(1)} %get-tuple-element.1615) | copy-start | bytes 3076
  30.3 34.9 %copy-start.12 = (s32[256]{0:T(256)}, s32[256]{0:T(256)S(1)}, u32[]{:S(2)}) copy-start(s32[256]{0:T(256)S(1)} %get-tuple-element.1663) | copy-start | bytes 3076
  30.3 38.8 %copy-start.7 = (s32[256]{0:T(256)}, s32[256]{0:T(256)S(1)}, u32[]{:S(2)}) copy-start(s32[256]{0:T(256)S(1)} %get-tuple-element.1519) | copy-start | bytes 3076
  30.3 38.8 %copy-start.9 = (s32[256]{0:T(256)}, s32[256]{0:T(256)S(1)}, u32[]{:S(2)}) copy-start(s32[256]{0:T(256)S(1)} %get-tuple-element.1567) | copy-start | bytes 3076
  30.4 34.8 %collective-permute-start = (bf16[2,1024,128]{2,1,0:T(8,128)(2,1)S(1)}, bf16[2,1024,128]{2,1,0:T(8,128)(2,1)S(1)}, u32[]{:S(2)}, u32[]{:S(2)}) collective-permute-start(bf16[2,1024,128]{2,1,0:T(8,128)(2,1)S(1)} %pad_maximum_fusion.1), channel_id=1, source_target_pairs={{0,16},{8,24},{16,32},{24,40},{32,48},{40,56},{48,64},{56,72},{64,... | collective-permute-start | bytes 1572872 | tf_op jit(solution)/shard_map/ppermute | solution.py:19
  33.9 35.1 %collective-permute-start.1 = (bf16[2,1024,128]{2,1,0:T(8,128)(2,1)S(1)}, bf16[2,1024,128]{2,1,0:T(8,128)(2,1)S(1)}, u32[]{:S(2)}, u32[]{:S(2)}) collective-permute-start(bf16[2,1024,128]{2,1,0:T(8,128)(2,1)S(1)} %pad_maximum_fusion.1), channel_id=1, source_target_pairs={{0,8},{8,16},{16,24},{24,32},{32,40},{40,48},{48,56},{56,64},{64,7... | collective-permute-start | bytes 1572872 | tf_op jit(solution)/shard_map/ppermute | solution.py:19
  83.7 1.3 copy-start.6
  142.8 1.7 copy-start.10
  166.4 1.7 copy-start.8
  184.7 1.0 copy-start.3
  184.7 1.2 copy-start.4
where the time goes:
time: 226 us; the launch traced here: 223 us
  waiting for transfers between devices  55.2 us (24%)
  matrix products  52.6 us (23%)
  local copies, waits for them, and re-layouts  45.3 us (20%)
  blocking collectives  29.6 us (13%)
  other arithmetic  19.5 us (9%)
  starting transfers between devices  18.7 us (8%)
    ppermute x2, waiting for transfers between devices, from_behind(): lax.ppermute(value, axis, [(source, source + steps) for source in range(l...  32.1 us
    all_to_all x1, blocking collectives, shards(): lax.all_to_all(local_out, 'head', split_axis=0, concat_axis=1, tiled=True)  29.6 us
    dot_general x24, matrix products, attend_tile(): jnp.einsum('qgjd,kgd->qgjk', query_block, key_tile, preferred_element_typ...  28.9 us
    dot_general x24, matrix products, attend_tile(): jnp.einsum('qgjk,kgd->qgjd', weights.astype(jnp.bfloat16), value_tile, pr...  23.6 us
    dynamic_slice x21, local copies, waits for them, and re-layouts, visit(): tile_ids = lax.dynamic_slice_in_dim(window_ids, start, BLOCK)  15.2 us
    unnamed x39, local copies, waits for them, and re-layouts  13.2 us
    all_to_all x1, waiting for transfers between devices, shards(): lax.all_to_all(queries, 'head', split_axis=1, concat_axis=0, tiled=True)  11.9 us
    and x22, other arithmetic, visit(): (block_ids[:, None] == tile_ids[None, :]) & (key_pos[None, :] <= query_po...  10.1 us
  transfers between devices with their start and end apart: 5, of which 5 were waited for; matrix products, arithmetic and copies ran while one was open for 4% of the time, Pallas kernels for 0%

commit v1 on v0

--- a/solution.py
+++ b/solution.py
@@ -52,7 +52,12 @@
     local_queries, local_keys, local_values = (
         lax.all_to_all(queries, "head", split_axis=1, concat_axis=0, tiled=True),
         lax.all_to_all(keys, "head", split_axis=1, concat_axis=0, tiled=True),
-        lax.all_to_all(values, "head", split_axis=1, concat_axis=0, tiled=True),
+        jnp.concatenate(
+            lax.all_to_all(
+                jnp.stack(jnp.split(values, lax.axis_size("head"), axis=1)), "head", 0, 0
+            ),
+            axis=0,
+        ),
     )
     window = key_window(jnp.stack([local_keys, local_values]))
     groups = local_keys.shape[1] // HD

time: 226 us -> 198 us (0.88)
  local copies, waits for them, and re-layouts: 45.3 us -> 34.4 us
  matrix products: 52.6 us -> 44 us
  other arithmetic: 19.5 us -> 13.3 us
  waiting for transfers between devices: 55.2 us -> 50.8 us
  starting transfers between devices: 18.7 us -> 21 us
    dynamic_slice x21, local copies, waits for them, and re-layouts: 15.2 us -> 1.65 us  [visit(): tile_ids = lax.dynamic_slice_in_dim(window_ids, start, BLOCK)]
    dot_general x24, matrix products: 23.6 us -> 15.8 us  [attend_tile(): jnp.einsum('qgjk,kgd->qgjd', weights.astype(jnp.bfloat16), value_tile, pr...]
    and x22, other arithmetic: 10.1 us -> 3.84 us  [visit(): (block_ids[:, None] == tile_ids[None, :]) & (key_pos[None, :] <= query_po...]
    all_to_all x1, waiting for transfers between devices: 5.59 us -> 0.01 us  [shards(): lax.all_to_all(keys, 'head', split_axis=1, concat_axis=0, tiled=True)]
    unnamed x39 -> x46, local copies, waits for them, and re-layouts: 13.2 us -> 16.9 us
    all_to_all x1, starting transfers between devices: 3.41 us -> 5.7 us  [shards(): lax.all_to_all(jnp.stack(jnp.split(values, lax.axis_size('head'), axis=1)...]
  transfers between devices with their start and end apart: 5 -> 5, of which waited for: 5 -> 4; matrix products, arithmetic and copies ran while one was open for 4% -> 8% of each run, Pallas kernels for 0% -> 0%
where the time goes in v1:
time: 198 us; the launch traced here: 196 us
  waiting for transfers between devices  50.8 us (26%)
  matrix products  44 us (22%)
  local copies, waits for them, and re-layouts  34.4 us (17%)
  blocking collectives  30.4 us (15%)
  starting transfers between devices  21 us (11%)
  other arithmetic  13.3 us (7%)
    ppermute x2, waiting for transfers between devices, from_behind(): lax.ppermute(value, axis, [(source, source + steps) for source in range(l...  32.7 us
    all_to_all x1, blocking collectives, shards(): lax.all_to_all(local_out, 'head', split_axis=0, concat_axis=1, tiled=True)  30.4 us
    dot_general x24, matrix products, attend_tile(): jnp.einsum('qgjd,kgd->qgjk', query_block, key_tile, preferred_element_typ...  28.1 us
    unnamed x46, local copies, waits for them, and re-layouts  16.9 us
    dot_general x24, matrix products, attend_tile(): jnp.einsum('qgjk,kgd->qgjd', weights.astype(jnp.bfloat16), value_tile, pr...  15.8 us
    all_to_all x1, waiting for transfers between devices, shards(): lax.all_to_all(queries, 'head', split_axis=1, concat_axis=0, tiled=True)  12.4 us
    reduce_sum x24, other arithmetic, attend_tile(): totals = totals * factor + jnp.sum(weights, axis=-1)  7.06 us
    all_to_all x2, local copies, waits for them, and re-layouts, shards(): lax.all_to_all(local_out, 'head', split_axis=0, concat_axis=1, tiled=True)  6.44 us
  transfers between devices with their start and end apart: 5, of which 4 were waited for; matrix products, arithmetic and copies ran while one was open for 8% of the time, Pallas kernels for 0%

profile of v1, /device:TPU:128, one launch (start us, length us, event | category | flops | bytes accessed | tf_op | source)
XLA Modules:
  0.0 195.8 jit_solution(15105151583968908754)
XLA Ops:
  1.7 6.1 %all-to-all-start = ((bf16[128,8,128]{2,0,1:T(8,128)(2,1)}), bf16[128,8,128]{2,0,1:T(8,128)(2,1)S(1)}, u32[]{:S(2)}, u32[]{:S(2)}) async-start(bf16[128,8,128]{2,0,1:T(8,128)(2,1)} %copy_bitcast_fusion.1), calls=%async_computation | async-start | bytes 524288 | tf_op jit(solution)/shard_map/all_to_all | solution.py:54
  7.8 1.4 bitcast_dynamic-update-slice_fusion.7
  9.2 1.4 bitcast_dynamic-update-slice_fusion.6
  10.5 1.4 bitcast_dynamic-update-slice_fusion.5
  11.9 1.4 bitcast_dynamic-update-slice_fusion.4
  13.3 1.4 bitcast_dynamic-update-slice_fusion.3
  14.6 1.4 bitcast_dynamic-update-slice_fusion.2
  16.0 1.4 bitcast_dynamic-update-slice_fusion.1
  17.3 1.4 bitcast_dynamic-update-slice_fusion
  18.7 5.7 %all-to-all-start.2 = ((bf16[8,128,128]{2,1,0:T(8,128)(2,1)}), bf16[8,128,128]{2,1,0:T(8,128)(2,1)S(1)}, u32[]{:S(2)}, u32[]{:S(2)}) async-start(bf16[8,128,128]{2,1,0:T(8,128)(2,1)} %bitcast_dynamic-update-slice_fusion), calls=%async_computation.2 | async-start | bytes 524288 | tf_op jit(solution)/shard_map/all_to_all | solution.py:56
  24.4 1.6 copy.132
  26.0 5.7 %all-to-all-done.2 = bf16[8,128,128]{2,1,0:T(8,128)(2,1)S(1)} async-done(((bf16[8,128,128]{2,1,0:T(8,128)(2,1)}), bf16[8,128,128]{2,1,0:T(8,128)(2,1)S(1)}, u32[]{:S(2)}, u32[]{:S(2)}) %all-to-all-start.2) | async-done | bytes 262176 | tf_op jit(solution)/shard_map/all_to_all | solution.py:56
  31.7 3.7 %all-to-all-start.1 = ((bf16[128,8,1024]{2,0,1:T(8,128)(2,1)}), bf16[128,8,1024]{2,0,1:T(8,128)(2,1)S(1)}, u32[]{:S(2)}, u32[]{:S(2)}) async-start(bf16[128,8,1024]{2,0,1:T(8,128)(2,1)} %bitcast.410), calls=%async_computation.1 | async-start | bytes 4194304 | tf_op jit(solution)/shard_map/all_to_all | solution.py:53
  35.8 3.5 %collective-permute-start = (bf16[2,1024,128]{2,1,0:T(8,128)(2,1)S(1)}, bf16[2,1024,128]{2,1,0:T(8,128)(2,1)S(1)}, u32[]{:S(2)}, u32[]{:S(2)}) collective-permute-start(bf16[2,1024,128]{2,1,0:T(8,128)(2,1)S(1)} %pad_maximum_fusion.1), channel_id=1, source_target_pairs={{0,16},{8,24},{16,32},{24,40},{32,48},{40,56},{48,64},{56,72},{64,... | collective-permute-start | bytes 1572872 | tf_op jit(solution)/shard_map/ppermute | solution.py:19
  39.3 1.9 collective-permute-start.1
  42.3 28.1 %collective-permute-done = bf16[2,1024,128]{2,1,0:T(8,128)(2,1)S(1)} collective-permute-done((bf16[2,1024,128]{2,1,0:T(8,128)(2,1)S(1)}, bf16[2,1024,128]{2,1,0:T(8,128)(2,1)S(1)}, u32[]{:S(2)}, u32[]{:S(2)}) %collective-permute-start) | collective-permute-done | bytes 524320 | tf_op jit(solution)/shard_map/ppermute | solution.py:19
  70.4 4.6 %collective-permute-done.1 = bf16[2,1024,128]{2,1,0:T(8,128)(2,1)S(1)} collective-permute-done((bf16[2,1024,128]{2,1,0:T(8,128)(2,1)S(1)}, bf16[2,1024,128]{2,1,0:T(8,128)(2,1)S(1)}, u32[]{:S(2)}, u32[]{:S(2)}) %collective-permute-start.1) | collective-permute-done | bytes 524320 | tf_op jit(solution)/shard_map/ppermute | solution.py:19
  75.1 1.3 slice_bitcast_fusion
  76.4 1.4 copy.62
  77.8 12.4 %all-to-all-done.1 = bf16[128,8,1024]{2,0,1:T(8,128)(2,1)S(1)} async-done(((bf16[128,8,1024]{2,0,1:T(8,128)(2,1)}), bf16[128,8,1024]{2,0,1:T(8,128)(2,1)S(1)}, u32[]{:S(2)}, u32[]{:S(2)}) %all-to-all-start.1) | async-done | bytes 2097184 | tf_op jit(solution)/shard_map/all_to_all | solution.py:53
  93.1 13.2 %while.72 = (s32[]{:T(128)}, f32[256,1,8]{0,2,1:T(8,128)S(1)}, f32[256,1,8]{0,2,1:T(8,128)S(1)}, f32[256,1,8,128]{0,3,2,1:T(8,128)S(1)}, s32[256]{0:T(256)S(1)},...) while((s32[]{:T(128)}, f32[256,1,8]{0,2,1:T(8,128)S(1)}, ...), condition=%wide.region_5.6_spmd.clone, body=%wide.region_2.5_spmd.clone.sunk | while | flops 272833024 | bytes 9314543 | solution.py:101
  93.5 1.3 fusion.145
  96.1 1.3 fusion.145
  98.7 1.3 fusion.145
  101.3 1.3 fusion.145
  103.9 1.3 fusion.145
  110.1 13.0 %while.73 = (s32[]{:T(128)}, f32[256,1,8]{0,2,1:T(8,128)S(1)}, f32[256,1,8]{0,2,1:T(8,128)S(1)}, f32[256,1,8,128]{0,3,2,1:T(8,128)S(1)}, s32[256]{0:T(256)S(1)},...) while((s32[]{:T(128)}, f32[256,1,8]{0,2,1:T(8,128)S(1)}, ...), condition=%wide.region_11.12_spmd.clone, body=%wide.region_8.11_spmd.clone.sunk | while | flops 272833024 | bytes 9314543 | solution.py:101
  110.3 1.3 fusion.151
  112.9 1.3 fusion.151
  115.5 1.3 fusion.151
  118.1 1.3 fusion.151
  120.7 1.3 fusion.151
  126.8 13.0 %while.74 = (s32[]{:T(128)}, f32[256,1,8]{0,2,1:T(8,128)S(1)}, f32[256,1,8]{0,2,1:T(8,128)S(1)}, f32[256,1,8,128]{0,3,2,1:T(8,128)S(1)}, s32[256]{0:T(256)S(1)},...) while((s32[]{:T(128)}, f32[256,1,8]{0,2,1:T(8,128)S(1)}, ...), condition=%wide.region_17.18_spmd.clone, body=%wide.region_14.17_spmd.clone.sunk | while | flops 272833024 | bytes 9314543 | solution.py:101
  127.0 1.3 fusion.157
  129.6 1.3 fusion.157
  132.2 1.3 fusion.157
  134.8 1.3 fusion.157
  137.5 1.3 fusion.157
  143.5 13.0 %while.75 = (s32[]{:T(128)}, f32[256,1,8]{0,2,1:T(8,128)S(1)}, f32[256,1,8]{0,2,1:T(8,128)S(1)}, f32[256,1,8,128]{0,3,2,1:T(8,128)S(1)}, s32[256]{0:T(256)S(1)},...) while((s32[]{:T(128)}, f32[256,1,8]{0,2,1:T(8,128)S(1)}, ...), condition=%wide.region_23.24_spmd.clone, body=%wide.region_20.23_spmd.clone.sunk | while | flops 272833024 | bytes 9314543 | solution.py:101
  143.7 1.3 fusion.163
  146.4 1.3 fusion.163
  149.0 1.3 fusion.163
  151.6 1.3 fusion.163
  154.2 1.3 fusion.163
  157.8 1.2 pad_maximum_fusion
  159.0 30.4 %all_to_all.56 = bf16[8,128,1024]{2,1,0:T(8,128)(2,1)S(1)} all-to-all(bf16[8,128,1024]{2,1,0:T(8,128)(2,1)S(1)} %bitcast.411), channel_id=1, replica_groups=mesh['ctx'=64,'head'=8] {'head'}, dimensions={0} | all-to-all | bytes 4194304 | tf_op jit(solution)/shard_map/all_to_all | solution.py:107
  189.4 2.4 %copy.82 = bf16[128,8,1024]{0,2,1:T(8,128)(2,1)} copy(bf16[128,8,1024]{2,0,1:T(8,128)(2,1)S(1)} %bitcast.412) | data formatting | bytes 4194304 | tf_op jit(solution)/shard_map/all_to_all | solution.py:107
  191.8 4.1 %copy.83 = bf16[128,8192]{1,0:T(8,128)(2,1)} copy(bf16[128,8192]{0,1:T(8,128)(2,1)} %bitcast.413) | data formatting | bytes 4194304 | tf_op jit(solution)/shard_map/all_to_all | solution.py:107
  (245 shorter events, 42.6 us)
Async XLA Ops:
  0.0 1.0 copy-start
  0.0 24.4 %copy-start.3 = (bf16[128,8192]{1,0:T(8,128)(2,1)S(1)}, bf16[128,8192]{1,0:T(8,128)(2,1)}, u32[]{:S(2)}) copy-start(bf16[128,8192]{1,0:T(8,128)(2,1)} %param.12) | copy-start | bytes 6291460
  1.7 17.0 %all-to-all-start = ((bf16[128,8,128]{2,0,1:T(8,128)(2,1)}), bf16[128,8,128]{2,0,1:T(8,128)(2,1)S(1)}, u32[]{:S(2)}, u32[]{:S(2)}) async-start(bf16[128,8,128]{2,0,1:T(8,128)(2,1)} %copy_bitcast_fusion.1), calls=%async_computation | async-start | bytes 524288 | tf_op jit(solution)/shard_map/all_to_all | solution.py:54
  18.7 13.0 %all-to-all-start.2 = ((bf16[8,128,128]{2,1,0:T(8,128)(2,1)}), bf16[8,128,128]{2,1,0:T(8,128)(2,1)S(1)}, u32[]{:S(2)}, u32[]{:S(2)}) async-start(bf16[8,128,128]{2,1,0:T(8,128)(2,1)} %bitcast_dynamic-update-slice_fusion), calls=%async_computation.2 | async-start | bytes 524288 | tf_op jit(solution)/shard_map/all_to_all | solution.py:56
  31.7 43.3 %copy-start.1 = (bf16[8,128,128]{2,1,0:T(8,128)(2,1)}, bf16[8,128,128]{2,1,0:T(8,128)(2,1)S(1)}, u32[]{:S(2)}) copy-start(bf16[8,128,128]{2,1,0:T(8,128)(2,1)S(1)} %all-to-all-done.2) | copy-start | bytes 786436
  31.7 3.8 %copy-start.6 = (s32[65536]{0:T(1024)S(1)}, s32[65536]{0:T(1024)}, u32[]{:S(2)}) copy-start(s32[65536]{0:T(1024)} %param.15) | copy-start | bytes 786436
  31.7 58.5 %all-to-all-start.1 = ((bf16[128,8,1024]{2,0,1:T(8,128)(2,1)}), bf16[128,8,1024]{2,0,1:T(8,128)(2,1)S(1)}, u32[]{:S(2)}, u32[]{:S(2)}) async-start(bf16[128,8,1024]{2,0,1:T(8,128)(2,1)} %bitcast.410), calls=%async_computation.1 | async-start | bytes 4194304 | tf_op jit(solution)/shard_map/all_to_all | solution.py:53
  35.7 6.4 %copy-start.11 = (s32[256]{0:T(256)}, s32[256]{0:T(256)S(1)}, u32[]{:S(2)}) copy-start(s32[256]{0:T(256)S(1)} %get-tuple-element.1615) | copy-start | bytes 3076
  35.7 6.4 %copy-start.13 = (s32[256]{0:T(256)}, s32[256]{0:T(256)S(1)}, u32[]{:S(2)}) copy-start(s32[256]{0:T(256)S(1)} %get-tuple-element.1663) | copy-start | bytes 3076
  35.7 34.7 %copy-start.9 = (s32[256]{0:T(256)}, s32[256]{0:T(256)S(1)}, u32[]{:S(2)}) copy-start(s32[256]{0:T(256)S(1)} %get-tuple-element.1567) | copy-start | bytes 3076
  35.8 34.6 %collective-permute-start = (bf16[2,1024,128]{2,1,0:T(8,128)(2,1)S(1)}, bf16[2,1024,128]{2,1,0:T(8,128)(2,1)S(1)}, u32[]{:S(2)}, u32[]{:S(2)}) collective-permute-start(bf16[2,1024,128]{2,1,0:T(8,128)(2,1)S(1)} %pad_maximum_fusion.1), channel_id=1, source_target_pairs={{0,16},{8,24},{16,32},{24,40},{32,48},{40,56},{48,64},{56,72},{64,... | collective-permute-start | bytes 1572872 | tf_op jit(solution)/shard_map/ppermute | solution.py:19
  39.3 35.7 %collective-permute-start.1 = (bf16[2,1024,128]{2,1,0:T(8,128)(2,1)S(1)}, bf16[2,1024,128]{2,1,0:T(8,128)(2,1)S(1)}, u32[]{:S(2)}, u32[]{:S(2)}) collective-permute-start(bf16[2,1024,128]{2,1,0:T(8,128)(2,1)S(1)} %pad_maximum_fusion.1), channel_id=1, source_target_pairs={{0,8},{8,16},{16,24},{24,32},{32,40},{40,48},{48,56},{56,64},{64,7... | collective-permute-start | bytes 1572872 | tf_op jit(solution)/shard_map/ppermute | solution.py:19
  90.2 1.3 copy-start.8
  91.5 1.0 copy-start.2
  92.4 0.7 copy-start.14
  106.3 2.3 %copy-start.7 = (pred[256,256]{0,1:T(8,128)(4,1)S(1)}, pred[256,256]{0,1:T(8,128)(4,1)}, u32[]{:S(2)}) copy-start(pred[256,256]{0,1:T(8,128)(4,1)} %get-tuple-element.1197) | copy-start | bytes 196612
  109.4 0.7 copy-start.12
  126.1 0.7 copy-start.10
  156.5 1.0 copy-start.4
  156.6 1.2 copy-start.5
